TPU v7x, 256 devices: a whole 4x4x8 slice. The times are simulated.
256 devices in a mesh: span: 8 (over y, x_hi), tm: 32 (over x_lo, z, core).
Axes of the slice: x: 4 (x_hi: 2, x_lo: 2; x = x_hi * 2 + x_lo), y: 4, z: 8, core: 2. Of those that a mesh axis runs over, the one named last changes fastest.
Arguments:
- launched: float32 [8, 2, 110, 8192], P(None, None, None, 'tm'), may hold values from -1.5 to 1.5
- coupling: float32 [8, 2, 2, 2, 110, 110], P('span'), may hold values from -2 to 2
- impulse: float32 [8, 2, 2, 2, 129], P('span'), may hold values from -1.5 to 1.5
- amplifier: float32 [8, 2, 110], P('span'), may hold values from 0.9 to 1.11
- nonlinear: float32 [8, 2, 2], P('span'), may hold values from 0.002 to 0.008
Outputs:
- monitored: float32 [8, 8, 2, 110, 8192], P('span', None, None, None, 'tm')
All inputs are finite; a program needn't handle non-finite values.
Results may differ from a plain program's by a relative error of at most 0.0004.
Values sent between devices are 32-bit elements; how exact they have to be, the bound alone decides.
No kernel may reach another device: no remote copies, remote signals or barrier semaphores. Data moves between devices by JAX's collectives and lax.ppermute only.
A program may use at most 64 MiB of HBM per device.

v0:
```python
import jax
import jax.numpy as jnp
from jax import lax
from jax.sharding import PartitionSpec as P


def band(values, width):
    padded = jnp.concatenate([values, jnp.zeros((width,), jnp.float32)])
    tiled = jnp.tile(padded, width)[: width * 2 * width]
    return tiled.reshape(width, 2 * width).T


def prepare(coupling_group, impulse_group):
    half_taps = (impulse_group.shape[-1] - 1) // 2
    width = 2 * half_taps

    def toeplitz(pair):
        real_band = band(pair[0], width)
        imag_band = band(pair[1], width)
        upper = jnp.concatenate([real_band, imag_band], axis=1)
        lower = jnp.concatenate([-imag_band, real_band], axis=1)
        return jnp.concatenate([upper, lower], axis=0)

    filters = jax.vmap(jax.vmap(toeplitz))(impulse_group)
    real_part = coupling_group[:, :, 0]
    imag_part = coupling_group[:, :, 1]
    upper = jnp.concatenate([real_part, -imag_part], axis=-1)
    lower = jnp.concatenate([imag_part, real_part], axis=-1)
    return (filters, jnp.concatenate([upper, lower], axis=-2))


def disperse(extended, matrix, half_taps):
    width = 2 * half_taps
    frames, _, channels, extent = extended.shape
    block_count = extent // width - 1
    blocks = extended.reshape(frames, 2, channels, block_count + 1, width)
    windows = jnp.concatenate([blocks[..., :-1, :], blocks[..., 1:, :]], axis=-1)
    stacked = jnp.concatenate([windows[:, 0], windows[:, 1]], axis=-1)
    product = jnp.einsum("fcbu,uv->fcbv", stacked, matrix, precision=lax.Precision.HIGHEST)
    real_part = product[..., :width].reshape(frames, channels, block_count * width)
    imag_part = product[..., width:].reshape(frames, channels, block_count * width)
    return jnp.stack([real_part, imag_part], axis=1)


def couple(signal, mixer, coefficient):
    frames, _, channels, extent = signal.shape
    flat = signal.reshape(frames, 2 * channels, extent)
    mixed = jnp.einsum("de,fel->fdl", mixer, flat, precision=lax.Precision.HIGHEST).reshape(
        frames, 2, channels, extent
    )
    power = jnp.sum(mixed * mixed, axis=(1, 2))
    phase = coefficient * power[:, None, :]
    cosine = jnp.cos(phase)
    sine = jnp.sin(phase)
    real_part = mixed[:, 0]
    imag_part = mixed[:, 1]
    return jnp.stack(
        [real_part * cosine - imag_part * sine, real_part * sine + imag_part * cosine], axis=1
    )


def neighbours(block, halo):
    count = lax.axis_size("tm")
    forward = [(i, i + 1) for i in range(count - 1)]
    backward = [(i + 1, i) for i in range(count - 1)]
    extent = block.shape[-1]
    low = lax.ppermute(lax.slice_in_dim(block, extent - halo, None, axis=3), "tm", forward)
    high = lax.ppermute(lax.slice_in_dim(block, 0, halo, axis=3), "tm", backward)
    return jnp.concatenate([low, block, high], axis=3)


def group_pass(signal, filters, mixers, amplifier_group, nonlinear_group, origin, length):
    span_count, step_count = nonlinear_group.shape
    half_taps = filters.shape[-1] // 4
    halo = span_count * step_count * half_taps
    extent = signal.shape[-1]
    signal = neighbours(signal, halo)
    offset = -halo
    for span_index in range(span_count):
        for step_index in range(step_count):
            signal = disperse(signal, filters[span_index, step_index], half_taps)
            offset = offset + half_taps
            where = origin + offset + jnp.arange(signal.shape[-1], dtype=jnp.int32)
            inside = ((where >= 0) & (where < length)).astype(jnp.float32)
            signal = signal * inside
            signal = couple(
                signal, mixers[span_index, step_index], nonlinear_group[span_index, step_index]
            )
        signal = signal * amplifier_group[span_index][None, None, :, None]
    assert signal.shape[-1] == extent
    return signal


def shards(launched, coupling, impulse, amplifier, nonlinear):
    sections = lax.axis_size("span")
    section_index = lax.axis_index("span")
    frames_count, _, _, extent = launched.shape
    per_section = frames_count // sections
    length = extent * lax.axis_size("tm")
    origin = lax.axis_index("tm") * extent
    coupling_all = lax.all_gather(coupling, "span", axis=0, tiled=True)
    impulse_all = lax.all_gather(impulse, "span", axis=0, tiled=True)
    amplifier_all = lax.all_gather(amplifier, "span", axis=0, tiled=True)
    nonlinear_all = lax.all_gather(nonlinear, "span", axis=0, tiled=True)
    signal = lax.dynamic_slice_in_dim(launched, section_index * per_section, per_section, 0)

    def advance(signal, params):
        coupling_group, impulse_group, amplifier_group, nonlinear_group = params
        filters, mixers = prepare(coupling_group, impulse_group)
        signal = group_pass(
            signal, filters, mixers, amplifier_group, nonlinear_group, origin, length
        )
        return (signal, signal)

    _, stacked = lax.scan(
        advance, signal, (coupling_all, impulse_all, amplifier_all, nonlinear_all)
    )
    return lax.all_to_all(stacked, "span", 0, 1, tiled=True)


def solution(mesh):
    placed = (
        P(None, None, None, "tm"),
        P("span", None, None, None, None, None),
        P("span", None, None, None, None),
        P("span", None, None),
        P("span", None, None),
    )
    return jax.shard_map(
        shards,
        mesh=mesh,
        in_specs=placed,
        out_specs=P("span", None, None, None, "tm"),
        check_vma=False,
    )
```

profile of v0, /device:TPU:2, one launch (start us, length us, event | category | flops | bytes accessed | tf_op | source)
XLA Modules:
  0.0 689.6 jit_solution(1994653478486105164)
XLA Ops:
  8.7 22.9 %all_gather.14 = f32[8,2,2]{2,1,0:T(2,128)S(1)} all-gather(f32[1,2,2]{2,1,0:T(2,128)} %param.11), channel_id=1, replica_groups=mesh['span'=8,'tm'=32] {'span'}, dimensions={0}, use_global_device_ids=true | all-gather | bytes 144 | tf_op jit(solution)/shard_map/all_gather | solution.py:104
  31.7 18.4 %all_gather.15 = f32[8,2,110]{2,1,0:T(2,128)S(1)} all-gather(f32[1,2,110]{2,1,0:T(2,128)} %param.10), channel_id=1, replica_groups=mesh['span'=8,'tm'=32] {'span'}, dimensions={0}, use_global_device_ids=true | all-gather | bytes 7920 | tf_op jit(solution)/shard_map/all_gather | solution.py:103
  50.1 37.0 %all_gather.12 = f32[8,2,2,2,129]{4,3,2,1,0:T(2,128)} all-gather(f32[1,2,2,2,129]{4,3,2,1,0:T(2,128)} %param.9), channel_id=1, replica_groups=mesh['span'=8,'tm'=32] {'span'}, dimensions={0}, use_global_device_ids=true | all-gather | bytes 37152 | tf_op jit(solution)/shard_map/all_gather | solution.py:102
  87.1 568.2 %while.13 = (s32[]{:T(128)}, f32[1,2,110,256]{3,2,1,0:T(8,128)}, f32[8,1,2,110,256]{4,2,3,1,0:T(2,128)}, f32[8,2,2,2,129]{4,3,2,1,0:T(2,128)}, s32[]{:T(128)}, /...) while((s32[]{:T(128)}, f32[1,2,110,256]{3,2,1,0:T(8,128)}, ...), condition=%wide.region_5.6_spmd, body=%wide.region_0.5_spmd.sunk | while | flops 3470978304 | bytes 83243504 | solution.py:115
  89.0 2.4 collective-permute-start.1
  101.0 2.3 reshape.881
  103.3 2.0 copy.116
  106.0 2.7 maximum_maximum_fusion.4
  109.1 2.1 pad_maximum_fusion.6
  115.1 2.2 copy.120
  118.4 2.1 convolution_bitcast_fusion.12
  138.9 2.4 multiply_reduce_fusion.9
  154.8 8.4 %collective-permute-start = (f32[1,2,110,256]{3,2,1,0:T(8,128)}, f32[1,2,110,256]{3,2,1,0:T(8,128)}, u32[]{:S(2)}, u32[]{:S(2)}) collective-permute-start(f32[1,2,110,256]{3,2,1,0:T(8,128)} %get-tuple-element.367), channel_id=1, source_target_pairs={{1,0},{2,1},{3,2},{4,3},{5,4},{6,5},{7,6},{8,7},{9,8},{10,9},{11,1... | collective-permute-start | bytes 675848 | tf_op jit(solution)/shard_map/while/body/eval_jaxpr/ppermute | solution.py:68
  174.7 2.3 reshape.881
  177.0 2.0 copy.116
  179.8 2.7 maximum_maximum_fusion.4
  182.8 2.1 pad_maximum_fusion.6
  188.8 2.2 copy.120
  192.1 2.1 convolution_bitcast_fusion.12
  212.6 2.4 multiply_reduce_fusion.9
  228.6 5.7 collective-permute-start
  245.8 2.3 reshape.881
  248.1 2.0 copy.116
  250.9 2.7 maximum_maximum_fusion.4
  253.9 2.1 pad_maximum_fusion.6
  259.9 2.2 copy.120
  263.2 2.1 convolution_bitcast_fusion.12
  283.7 2.4 multiply_reduce_fusion.9
  299.7 5.7 collective-permute-start
  316.9 2.3 reshape.881
  322.0 2.7 maximum_maximum_fusion.4
  325.0 2.1 pad_maximum_fusion.6
  331.0 2.2 copy.120
  334.3 2.1 convolution_bitcast_fusion.12
  354.8 2.4 multiply_reduce_fusion.9
  370.8 5.7 collective-permute-start
  388.0 2.3 reshape.881
  393.1 2.7 maximum_maximum_fusion.4
  396.1 2.1 pad_maximum_fusion.6
  402.1 2.2 copy.120
  405.4 2.1 convolution_bitcast_fusion.12
  426.0 2.4 multiply_reduce_fusion.9
  441.9 5.7 collective-permute-start
  459.1 2.3 reshape.881
  464.2 2.7 maximum_maximum_fusion.4
  467.2 2.1 pad_maximum_fusion.6
  473.2 2.2 copy.120
  476.5 2.1 convolution_bitcast_fusion.12
  497.1 2.4 multiply_reduce_fusion.9
  513.0 5.7 collective-permute-start
  530.3 2.3 reshape.881
  535.3 2.7 maximum_maximum_fusion.4
  538.3 2.1 pad_maximum_fusion.6
  544.3 2.2 copy.120
  547.6 2.1 convolution_bitcast_fusion.12
  568.2 2.4 multiply_reduce_fusion.9
  584.1 5.7 collective-permute-start
  601.4 2.3 reshape.881
  606.4 2.7 maximum_maximum_fusion.4
  609.4 2.1 pad_maximum_fusion.6
  615.4 2.2 copy.120
  618.7 2.1 convolution_bitcast_fusion.12
  639.3 2.4 multiply_reduce_fusion.9
  655.2 26.3 %all_to_all.12 = f32[8,1,2,110,256]{4,2,3,1,0:T(2,128)S(1)} all-to-all(f32[8,1,2,110,256]{4,2,3,1,0:T(2,128)} %get-tuple-element.90), channel_id=1, replica_groups=mesh['span'=8,'tm'=32] {'span'}, dimensions={0} | all-to-all | bytes 3604480 | tf_op jit(solution)/shard_map/all_to_all | solution.py:118
  (862 shorter events, 406.6 us)
Async XLA Ops:
  6.5 1.5 copy-start
  6.5 80.5 %all-gather.2.cloned.1.call-start = ((), (), s32[]{:S(2)}) async-start(), calls=%async_computation.1 | async-start | bytes 4055040 | tf_op jit(solution)/shard_map/all_gather | solution.py:101
  87.1 22.0 %collective-permute-start = (f32[1,2,110,256]{3,2,1,0:T(8,128)}, f32[1,2,110,256]{3,2,1,0:T(8,128)}, u32[]{:S(2)}, u32[]{:S(2)}) collective-permute-start(f32[1,2,110,256]{3,2,1,0:T(8,128)} %get-tuple-element.367), channel_id=1, source_target_pairs={{1,0},{2,1},{3,2},{4,3},{5,4},{6,5},{7,6},{8,7},{9,8},{10,9},{11,1... | collective-permute-start | bytes 675848 | tf_op jit(solution)/shard_map/while/body/eval_jaxpr/ppermute | solution.py:68
  89.0 20.1 %collective-permute-start.1 = (f32[1,2,110,256]{3,2,1,0:T(8,128)}, f32[1,2,110,256]{3,2,1,0:T(8,128)}, u32[]{:S(2)}, u32[]{:S(2)}) collective-permute-start(f32[1,2,110,256]{3,2,1,0:T(8,128)} %get-tuple-element.367), channel_id=1, source_target_pairs={{0,1},{1,2},{2,3},{3,4},{4,5},{5,6},{6,7},{7,8},{8,9},{9,10},{10,1... | collective-permute-start | bytes 675848 | tf_op jit(solution)/shard_map/while/body/eval_jaxpr/ppermute | solution.py:67
  99.1 7.0 %copy-start.1 = (f32[2,2,256,128]{3,2,1,0:T(8,128)S(1)}, f32[2,2,256,128]{3,2,1,0:T(8,128)}, u32[]{:S(2)}) copy-start(f32[2,2,256,128]{3,2,1,0:T(8,128)} %bitcast_negate_fusion.2) | copy-start | bytes 1572868 | tf_op jit(solution)/shard_map/while
  105.4 3.3 copy-start.2
  105.4 3.3 copy-start.3
  105.4 3.3 copy-start.4
  154.8 27.9 %collective-permute-start = (f32[1,2,110,256]{3,2,1,0:T(8,128)}, f32[1,2,110,256]{3,2,1,0:T(8,128)}, u32[]{:S(2)}, u32[]{:S(2)}) collective-permute-start(f32[1,2,110,256]{3,2,1,0:T(8,128)} %get-tuple-element.367), channel_id=1, source_target_pairs={{1,0},{2,1},{3,2},{4,3},{5,4},{6,5},{7,6},{8,7},{9,8},{10,9},{11,1... | collective-permute-start | bytes 675848 | tf_op jit(solution)/shard_map/while/body/eval_jaxpr/ppermute | solution.py:68
  163.2 19.6 %collective-permute-start.1 = (f32[1,2,110,256]{3,2,1,0:T(8,128)}, f32[1,2,110,256]{3,2,1,0:T(8,128)}, u32[]{:S(2)}, u32[]{:S(2)}) collective-permute-start(f32[1,2,110,256]{3,2,1,0:T(8,128)} %get-tuple-element.367), channel_id=1, source_target_pairs={{0,1},{1,2},{2,3},{3,4},{4,5},{5,6},{6,7},{7,8},{8,9},{9,10},{10,1... | collective-permute-start | bytes 675848 | tf_op jit(solution)/shard_map/while/body/eval_jaxpr/ppermute | solution.py:67
  172.8 7.0 %copy-start.1 = (f32[2,2,256,128]{3,2,1,0:T(8,128)S(1)}, f32[2,2,256,128]{3,2,1,0:T(8,128)}, u32[]{:S(2)}) copy-start(f32[2,2,256,128]{3,2,1,0:T(8,128)} %bitcast_negate_fusion.2) | copy-start | bytes 1572868 | tf_op jit(solution)/shard_map/while
  179.1 3.3 copy-start.2
  179.1 3.3 copy-start.3
  179.1 3.3 copy-start.4
  228.6 25.3 %collective-permute-start = (f32[1,2,110,256]{3,2,1,0:T(8,128)}, f32[1,2,110,256]{3,2,1,0:T(8,128)}, u32[]{:S(2)}, u32[]{:S(2)}) collective-permute-start(f32[1,2,110,256]{3,2,1,0:T(8,128)} %get-tuple-element.367), channel_id=1, source_target_pairs={{1,0},{2,1},{3,2},{4,3},{5,4},{6,5},{7,6},{8,7},{9,8},{10,9},{11,1... | collective-permute-start | bytes 675848 | tf_op jit(solution)/shard_map/while/body/eval_jaxpr/ppermute | solution.py:68
  234.3 19.6 %collective-permute-start.1 = (f32[1,2,110,256]{3,2,1,0:T(8,128)}, f32[1,2,110,256]{3,2,1,0:T(8,128)}, u32[]{:S(2)}, u32[]{:S(2)}) collective-permute-start(f32[1,2,110,256]{3,2,1,0:T(8,128)} %get-tuple-element.367), channel_id=1, source_target_pairs={{0,1},{1,2},{2,3},{3,4},{4,5},{5,6},{6,7},{7,8},{8,9},{9,10},{10,1... | collective-permute-start | bytes 675848 | tf_op jit(solution)/shard_map/while/body/eval_jaxpr/ppermute | solution.py:67
  243.9 7.0 %copy-start.1 = (f32[2,2,256,128]{3,2,1,0:T(8,128)S(1)}, f32[2,2,256,128]{3,2,1,0:T(8,128)}, u32[]{:S(2)}) copy-start(f32[2,2,256,128]{3,2,1,0:T(8,128)} %bitcast_negate_fusion.2) | copy-start | bytes 1572868 | tf_op jit(solution)/shard_map/while
  250.2 3.3 copy-start.2
  250.2 3.3 copy-start.3
  250.2 3.3 copy-start.4
  299.7 25.3 %collective-permute-start = (f32[1,2,110,256]{3,2,1,0:T(8,128)}, f32[1,2,110,256]{3,2,1,0:T(8,128)}, u32[]{:S(2)}, u32[]{:S(2)}) collective-permute-start(f32[1,2,110,256]{3,2,1,0:T(8,128)} %get-tuple-element.367), channel_id=1, source_target_pairs={{1,0},{2,1},{3,2},{4,3},{5,4},{6,5},{7,6},{8,7},{9,8},{10,9},{11,1... | collective-permute-start | bytes 675848 | tf_op jit(solution)/shard_map/while/body/eval_jaxpr/ppermute | solution.py:68
  305.4 19.6 %collective-permute-start.1 = (f32[1,2,110,256]{3,2,1,0:T(8,128)}, f32[1,2,110,256]{3,2,1,0:T(8,128)}, u32[]{:S(2)}, u32[]{:S(2)}) collective-permute-start(f32[1,2,110,256]{3,2,1,0:T(8,128)} %get-tuple-element.367), channel_id=1, source_target_pairs={{0,1},{1,2},{2,3},{3,4},{4,5},{5,6},{6,7},{7,8},{8,9},{9,10},{10,1... | collective-permute-start | bytes 675848 | tf_op jit(solution)/shard_map/while/body/eval_jaxpr/ppermute | solution.py:67
  315.0 7.0 %copy-start.1 = (f32[2,2,256,128]{3,2,1,0:T(8,128)S(1)}, f32[2,2,256,128]{3,2,1,0:T(8,128)}, u32[]{:S(2)}) copy-start(f32[2,2,256,128]{3,2,1,0:T(8,128)} %bitcast_negate_fusion.2) | copy-start | bytes 1572868 | tf_op jit(solution)/shard_map/while
  321.3 3.3 copy-start.2
  321.3 3.3 copy-start.3
  321.3 3.3 copy-start.4
  370.8 25.3 %collective-permute-start = (f32[1,2,110,256]{3,2,1,0:T(8,128)}, f32[1,2,110,256]{3,2,1,0:T(8,128)}, u32[]{:S(2)}, u32[]{:S(2)}) collective-permute-start(f32[1,2,110,256]{3,2,1,0:T(8,128)} %get-tuple-element.367), channel_id=1, source_target_pairs={{1,0},{2,1},{3,2},{4,3},{5,4},{6,5},{7,6},{8,7},{9,8},{10,9},{11,1... | collective-permute-start | bytes 675848 | tf_op jit(solution)/shard_map/while/body/eval_jaxpr/ppermute | solution.py:68
  376.5 19.6 %collective-permute-start.1 = (f32[1,2,110,256]{3,2,1,0:T(8,128)}, f32[1,2,110,256]{3,2,1,0:T(8,128)}, u32[]{:S(2)}, u32[]{:S(2)}) collective-permute-start(f32[1,2,110,256]{3,2,1,0:T(8,128)} %get-tuple-element.367), channel_id=1, source_target_pairs={{0,1},{1,2},{2,3},{3,4},{4,5},{5,6},{6,7},{7,8},{8,9},{9,10},{10,1... | collective-permute-start | bytes 675848 | tf_op jit(solution)/shard_map/while/body/eval_jaxpr/ppermute | solution.py:67
  386.1 7.0 %copy-start.1 = (f32[2,2,256,128]{3,2,1,0:T(8,128)S(1)}, f32[2,2,256,128]{3,2,1,0:T(8,128)}, u32[]{:S(2)}) copy-start(f32[2,2,256,128]{3,2,1,0:T(8,128)} %bitcast_negate_fusion.2) | copy-start | bytes 1572868 | tf_op jit(solution)/shard_map/while
  392.4 3.3 copy-start.2
  392.4 3.3 copy-start.3
  392.4 3.3 copy-start.4
  441.9 25.3 %collective-permute-start = (f32[1,2,110,256]{3,2,1,0:T(8,128)}, f32[1,2,110,256]{3,2,1,0:T(8,128)}, u32[]{:S(2)}, u32[]{:S(2)}) collective-permute-start(f32[1,2,110,256]{3,2,1,0:T(8,128)} %get-tuple-element.367), channel_id=1, source_target_pairs={{1,0},{2,1},{3,2},{4,3},{5,4},{6,5},{7,6},{8,7},{9,8},{10,9},{11,1... | collective-permute-start | bytes 675848 | tf_op jit(solution)/shard_map/while/body/eval_jaxpr/ppermute | solution.py:68
  447.6 19.6 %collective-permute-start.1 = (f32[1,2,110,256]{3,2,1,0:T(8,128)}, f32[1,2,110,256]{3,2,1,0:T(8,128)}, u32[]{:S(2)}, u32[]{:S(2)}) collective-permute-start(f32[1,2,110,256]{3,2,1,0:T(8,128)} %get-tuple-element.367), channel_id=1, source_target_pairs={{0,1},{1,2},{2,3},{3,4},{4,5},{5,6},{6,7},{7,8},{8,9},{9,10},{10,1... | collective-permute-start | bytes 675848 | tf_op jit(solution)/shard_map/while/body/eval_jaxpr/ppermute | solution.py:67
  457.2 7.0 %copy-start.1 = (f32[2,2,256,128]{3,2,1,0:T(8,128)S(1)}, f32[2,2,256,128]{3,2,1,0:T(8,128)}, u32[]{:S(2)}) copy-start(f32[2,2,256,128]{3,2,1,0:T(8,128)} %bitcast_negate_fusion.2) | copy-start | bytes 1572868 | tf_op jit(solution)/shard_map/while
  463.5 3.3 copy-start.2
  463.5 3.3 copy-start.3
  463.5 3.3 copy-start.4
  513.0 25.3 %collective-permute-start = (f32[1,2,110,256]{3,2,1,0:T(8,128)}, f32[1,2,110,256]{3,2,1,0:T(8,128)}, u32[]{:S(2)}, u32[]{:S(2)}) collective-permute-start(f32[1,2,110,256]{3,2,1,0:T(8,128)} %get-tuple-element.367), channel_id=1, source_target_pairs={{1,0},{2,1},{3,2},{4,3},{5,4},{6,5},{7,6},{8,7},{9,8},{10,9},{11,1... | collective-permute-start | bytes 675848 | tf_op jit(solution)/shard_map/while/body/eval_jaxpr/ppermute | solution.py:68
  518.8 19.6 %collective-permute-start.1 = (f32[1,2,110,256]{3,2,1,0:T(8,128)}, f32[1,2,110,256]{3,2,1,0:T(8,128)}, u32[]{:S(2)}, u32[]{:S(2)}) collective-permute-start(f32[1,2,110,256]{3,2,1,0:T(8,128)} %get-tuple-element.367), channel_id=1, source_target_pairs={{0,1},{1,2},{2,3},{3,4},{4,5},{5,6},{6,7},{7,8},{8,9},{9,10},{10,1... | collective-permute-start | bytes 675848 | tf_op jit(solution)/shard_map/while/body/eval_jaxpr/ppermute | solution.py:67
  528.3 7.0 %copy-start.1 = (f32[2,2,256,128]{3,2,1,0:T(8,128)S(1)}, f32[2,2,256,128]{3,2,1,0:T(8,128)}, u32[]{:S(2)}) copy-start(f32[2,2,256,128]{3,2,1,0:T(8,128)} %bitcast_negate_fusion.2) | copy-start | bytes 1572868 | tf_op jit(solution)/shard_map/while
  534.6 3.3 copy-start.2
  534.6 3.3 copy-start.3
  534.6 3.3 copy-start.4
  584.1 25.3 %collective-permute-start = (f32[1,2,110,256]{3,2,1,0:T(8,128)}, f32[1,2,110,256]{3,2,1,0:T(8,128)}, u32[]{:S(2)}, u32[]{:S(2)}) collective-permute-start(f32[1,2,110,256]{3,2,1,0:T(8,128)} %get-tuple-element.367), channel_id=1, source_target_pairs={{1,0},{2,1},{3,2},{4,3},{5,4},{6,5},{7,6},{8,7},{9,8},{10,9},{11,1... | collective-permute-start | bytes 675848 | tf_op jit(solution)/shard_map/while/body/eval_jaxpr/ppermute | solution.py:68
  589.9 19.6 %collective-permute-start.1 = (f32[1,2,110,256]{3,2,1,0:T(8,128)}, f32[1,2,110,256]{3,2,1,0:T(8,128)}, u32[]{:S(2)}, u32[]{:S(2)}) collective-permute-start(f32[1,2,110,256]{3,2,1,0:T(8,128)} %get-tuple-element.367), channel_id=1, source_target_pairs={{0,1},{1,2},{2,3},{3,4},{4,5},{5,6},{6,7},{7,8},{8,9},{9,10},{10,1... | collective-permute-start | bytes 675848 | tf_op jit(solution)/shard_map/while/body/eval_jaxpr/ppermute | solution.py:67
  599.4 7.0 %copy-start.1 = (f32[2,2,256,128]{3,2,1,0:T(8,128)S(1)}, f32[2,2,256,128]{3,2,1,0:T(8,128)}, u32[]{:S(2)}) copy-start(f32[2,2,256,128]{3,2,1,0:T(8,128)} %bitcast_negate_fusion.2) | copy-start | bytes 1572868 | tf_op jit(solution)/shard_map/while
  605.7 3.3 copy-start.2
  605.7 3.3 copy-start.3
  605.7 3.3 copy-start.4
Sparse Core Ops, SparseCore 0:
  9.9 74.1 all-gather.1
where the time goes:
time: 698 us; the launch traced here: 690 us
  local copies, waits for them, and re-layouts  275 us (39%)
  other arithmetic  132 us (19%)
  blocking collectives  105 us (15%)
  matrix products  98.7 us (14%)
  starting transfers between devices  60.5 us (9%)
  between operations  13.4 us (2%)
    dot_general x32, matrix products, disperse(): jnp.einsum('fcbu,uv->fcbv', stacked, matrix, precision=lax.Precision.HIGH...  59.1 us
    ppermute x8, starting transfers between devices, neighbours(): lax.ppermute(lax.slice_in_dim(block, 0, halo, axis=3), 'tm', backward)  44.6 us
    reshape x32, local copies, waits for them, and re-layouts, band(): return tiled.reshape(width, 2 * width).T  40 us
    dot_general x32, matrix products, couple(): jnp.einsum('de,fel->fdl', mixer, flat, precision=lax.Precision.HIGHEST)  39.6 us
    all_gather x1, blocking collectives, shards(): impulse_all = lax.all_gather(impulse, 'span', axis=0, tiled=True)  37 us
    while x80, local copies, waits for them, and re-layouts  28.2 us
    all_to_all x1, blocking collectives, shards(): return lax.all_to_all(stacked, 'span', 0, 1, tiled=True)  26.3 us
    mul x32, other arithmetic, group_pass(): signal = signal * inside  26.3 us
  transfers between devices with their start and end apart: 17, of which 0 were waited for; matrix products, arithmetic and copies ran while one was open for 20% of the time, Pallas kernels for 0%

commit v1 on v0

--- a/solution.py
+++ b/solution.py
@@ -2,6 +2,13 @@
 import jax.numpy as jnp
 from jax import lax
 from jax.sharding import PartitionSpec as P
+from jax.lax import all_to_all, axis_size
+
+
+def replace_the_bands(buf):
+    return jnp.concatenate(
+        all_to_all(jnp.stack(jnp.split(buf, axis_size("span"), axis=0)), "span", 0, 0), axis=1
+    )
 
 
 def band(values, width):
@@ -115,7 +122,7 @@
     _, stacked = lax.scan(
         advance, signal, (coupling_all, impulse_all, amplifier_all, nonlinear_all)
     )
-    return lax.all_to_all(stacked, "span", 0, 1, tiled=True)
+    return replace_the_bands(stacked)
 
 
 def solution(mesh):

time: 698 us -> 673 us (0.964)
  local copies, waits for them, and re-layouts: 275 us -> 259 us
  other arithmetic: 132 us -> 125 us
    reshape x32, local copies, waits for them, and re-layouts: 40 us -> 25.1 us  [band(): return tiled.reshape(width, 2 * width).T]
    concatenate x8, other arithmetic: 21.3 us -> 11.9 us  [toeplitz(): return jnp.concatenate([upper, lower], axis=0)]
  transfers between devices with their start and end apart: 17 -> 17, of which waited for: 0 -> 0; matrix products, arithmetic and copies ran while one was open for 20% -> 17% of each run, Pallas kernels for 0% -> 0%
where the time goes in v1:
time: 673 us; the launch traced here: 665 us
  local copies, waits for them, and re-layouts  259 us (38%)
  other arithmetic  125 us (19%)
  blocking collectives  104 us (15%)
  matrix products  98.5 us (15%)
  starting transfers between devices  60.6 us (9%)
  between operations  13.5 us (2%)
    dot_general x32, matrix products, disperse(): jnp.einsum('fcbu,uv->fcbv', stacked, matrix, precision=lax.Precision.HIGH...  59 us
    ppermute x8, starting transfers between devices, neighbours(): lax.ppermute(lax.slice_in_dim(block, 0, halo, axis=3), 'tm', backward)  44.8 us
    dot_general x32, matrix products, couple(): jnp.einsum('de,fel->fdl', mixer, flat, precision=lax.Precision.HIGHEST)  39.6 us
    all_gather x1, blocking collectives, shards(): impulse_all = lax.all_gather(impulse, 'span', axis=0, tiled=True)  37 us
    while x80, local copies, waits for them, and re-layouts  28.3 us
    mul x32, other arithmetic, group_pass(): signal = signal * inside  26.3 us
    all_to_all x1, blocking collectives, replace_the_bands(): all_to_all(jnp.stack(jnp.split(buf, axis_size('span'), axis=0)), 'span',...  26.1 us
    mul x48, local copies, waits for them, and re-layouts, group_pass(): signal = signal * inside  26.1 us
  transfers between devices with their start and end apart: 17, of which 0 were waited for; matrix products, arithmetic and copies ran while one was open for 17% of the time, Pallas kernels for 0%

profile of v1, /device:TPU:2, one launch (start us, length us, event | category | flops | bytes accessed | tf_op | source)
XLA Modules:
  0.0 665.1 jit_solution(11647246389389233629)
XLA Ops:
  8.8 22.9 %all_gather.14 = f32[8,2,2]{2,1,0:T(2,128)S(1)} all-gather(f32[1,2,2]{2,1,0:T(2,128)} %param.11), channel_id=1, replica_groups=mesh['span'=8,'tm'=32] {'span'}, dimensions={0}, use_global_device_ids=true | all-gather | bytes 144 | tf_op jit(solution)/shard_map/all_gather | solution.py:111
  31.7 18.4 %all_gather.15 = f32[8,2,110]{2,1,0:T(2,128)S(1)} all-gather(f32[1,2,110]{2,1,0:T(2,128)} %param.10), channel_id=1, replica_groups=mesh['span'=8,'tm'=32] {'span'}, dimensions={0}, use_global_device_ids=true | all-gather | bytes 7920 | tf_op jit(solution)/shard_map/all_gather | solution.py:110
  50.2 37.0 %all_gather.12 = f32[8,2,2,2,129]{4,3,2,1,0:T(2,128)} all-gather(f32[1,2,2,2,129]{4,3,2,1,0:T(2,128)} %param.9), channel_id=1, replica_groups=mesh['span'=8,'tm'=32] {'span'}, dimensions={0}, use_global_device_ids=true | all-gather | bytes 37152 | tf_op jit(solution)/shard_map/all_gather | solution.py:109
  87.1 539.6 %while.13 = (s32[]{:T(128)}, f32[1,2,110,256]{3,2,1,0:T(8,128)}, f32[8,1,2,110,256]{4,2,3,1,0:T(2,128)}, f32[8,2,2,2,129]{4,3,2,1,0:T(2,128)}, s32[]{:T(128)}, /...) while((s32[]{:T(128)}, f32[1,2,110,256]{3,2,1,0:T(8,128)}, ...), condition=%wide.region_5.6_spmd, body=%wide.region_0.5_spmd.sunk | while | flops 3470978304 | bytes 83243504 | solution.py:122
  87.1 1.9 collective-permute-start
  89.0 2.4 collective-permute-start.1
  105.3 2.1 pad_maximum_fusion.6
  111.4 2.2 copy.141
  114.7 2.1 convolution_bitcast_fusion.12
  127.7 1.9 copy.148
  130.9 1.9 convolution_bitcast_fusion.13
  135.2 2.4 multiply_reduce_fusion.9
  151.3 8.4 %collective-permute-start = (f32[1,2,110,256]{3,2,1,0:T(8,128)}, f32[1,2,110,256]{3,2,1,0:T(8,128)}, u32[]{:S(2)}, u32[]{:S(2)}) collective-permute-start(f32[1,2,110,256]{3,2,1,0:T(8,128)} %get-tuple-element.367), channel_id=1, source_target_pairs={{1,0},{2,1},{3,2},{4,3},{5,4},{6,5},{7,6},{8,7},{9,8},{10,9},{11,1... | collective-permute-start | bytes 675848 | tf_op jit(solution)/shard_map/while/body/eval_jaxpr/ppermute | solution.py:75
  159.7 1.9 collective-permute-start.1
  175.5 2.1 pad_maximum_fusion.6
  181.5 2.2 copy.141
  184.8 2.1 convolution_bitcast_fusion.12
  197.9 1.9 copy.148
  201.1 1.9 convolution_bitcast_fusion.13
  205.4 2.4 multiply_reduce_fusion.9
  221.5 5.7 collective-permute-start
  227.2 1.9 collective-permute-start.1
  243.0 2.1 pad_maximum_fusion.6
  249.1 2.2 copy.141
  252.4 2.1 convolution_bitcast_fusion.12
  265.4 1.9 copy.148
  268.6 1.9 convolution_bitcast_fusion.13
  272.9 2.4 multiply_reduce_fusion.9
  289.0 5.7 collective-permute-start
  294.8 1.9 collective-permute-start.1
  310.6 2.1 pad_maximum_fusion.6
  316.6 2.2 copy.141
  319.9 2.1 convolution_bitcast_fusion.12
  336.2 1.9 convolution_bitcast_fusion.13
  340.5 2.4 multiply_reduce_fusion.9
  356.6 5.7 collective-permute-start
  362.3 1.9 collective-permute-start.1
  378.1 2.1 pad_maximum_fusion.6
  384.2 2.2 copy.141
  387.5 2.1 convolution_bitcast_fusion.12
  403.7 1.9 convolution_bitcast_fusion.13
  408.0 2.4 multiply_reduce_fusion.9
  424.1 5.7 collective-permute-start
  429.9 1.9 collective-permute-start.1
  445.7 2.1 pad_maximum_fusion.6
  451.7 2.2 copy.141
  455.0 2.1 convolution_bitcast_fusion.12
  471.3 1.9 convolution_bitcast_fusion.13
  475.6 2.4 multiply_reduce_fusion.9
  491.7 5.7 collective-permute-start
  497.4 1.9 collective-permute-start.1
  513.2 2.1 pad_maximum_fusion.6
  519.2 2.2 copy.141
  522.5 2.1 convolution_bitcast_fusion.12
  538.8 1.9 convolution_bitcast_fusion.13
  543.1 2.4 multiply_reduce_fusion.9
  559.2 5.7 collective-permute-start
  565.0 1.9 collective-permute-start.1
  580.8 2.1 pad_maximum_fusion.6
  586.8 2.2 copy.141
  590.1 2.1 convolution_bitcast_fusion.12
  606.4 1.9 convolution_bitcast_fusion.13
  610.7 2.4 multiply_reduce_fusion.9
  630.9 26.1 %all_to_all.5 = f32[8,1,1,2,110,256]{5,3,4,2,1,0:T(2,128)S(1)} all-to-all(f32[8,1,1,2,110,256]{5,3,4,2,1,0:T(2,128)S(1)} %bitcast_dynamic-update-slice_fusion), channel_id=1, replica_groups=mesh['span'=8,'tm'=32] {'span'}, dimensions={0} | all-to-all | bytes 3604480 | tf_op jit(solution)/shard_map/all_to_all | solution.py:10
  (872 shorter events, 391.5 us)
Async XLA Ops:
  6.5 1.5 copy-start
  6.5 80.6 %all-gather.2.cloned.1.call-start = ((), (), s32[]{:S(2)}) async-start(), calls=%async_computation.1 | async-start | bytes 4055040 | tf_op jit(solution)/shard_map/all_gather | solution.py:108
  87.1 18.2 %collective-permute-start = (f32[1,2,110,256]{3,2,1,0:T(8,128)}, f32[1,2,110,256]{3,2,1,0:T(8,128)}, u32[]{:S(2)}, u32[]{:S(2)}) collective-permute-start(f32[1,2,110,256]{3,2,1,0:T(8,128)} %get-tuple-element.367), channel_id=1, source_target_pairs={{1,0},{2,1},{3,2},{4,3},{5,4},{6,5},{7,6},{8,7},{9,8},{10,9},{11,1... | collective-permute-start | bytes 675848 | tf_op jit(solution)/shard_map/while/body/eval_jaxpr/ppermute | solution.py:75
  89.0 16.3 %collective-permute-start.1 = (f32[1,2,110,256]{3,2,1,0:T(8,128)}, f32[1,2,110,256]{3,2,1,0:T(8,128)}, u32[]{:S(2)}, u32[]{:S(2)}) collective-permute-start(f32[1,2,110,256]{3,2,1,0:T(8,128)} %get-tuple-element.367), channel_id=1, source_target_pairs={{0,1},{1,2},{2,3},{3,4},{4,5},{5,6},{6,7},{7,8},{8,9},{9,10},{10,1... | collective-permute-start | bytes 675848 | tf_op jit(solution)/shard_map/while/body/eval_jaxpr/ppermute | solution.py:74
  99.1 4.4 copy-start.1
  103.4 1.5 copy-start.2
  103.4 1.5 copy-start.3
  103.4 1.5 copy-start.4
  151.3 24.2 %collective-permute-start = (f32[1,2,110,256]{3,2,1,0:T(8,128)}, f32[1,2,110,256]{3,2,1,0:T(8,128)}, u32[]{:S(2)}, u32[]{:S(2)}) collective-permute-start(f32[1,2,110,256]{3,2,1,0:T(8,128)} %get-tuple-element.367), channel_id=1, source_target_pairs={{1,0},{2,1},{3,2},{4,3},{5,4},{6,5},{7,6},{8,7},{9,8},{10,9},{11,1... | collective-permute-start | bytes 675848 | tf_op jit(solution)/shard_map/while/body/eval_jaxpr/ppermute | solution.py:75
  159.7 15.8 %collective-permute-start.1 = (f32[1,2,110,256]{3,2,1,0:T(8,128)}, f32[1,2,110,256]{3,2,1,0:T(8,128)}, u32[]{:S(2)}, u32[]{:S(2)}) collective-permute-start(f32[1,2,110,256]{3,2,1,0:T(8,128)} %get-tuple-element.367), channel_id=1, source_target_pairs={{0,1},{1,2},{2,3},{3,4},{4,5},{5,6},{6,7},{7,8},{8,9},{9,10},{10,1... | collective-permute-start | bytes 675848 | tf_op jit(solution)/shard_map/while/body/eval_jaxpr/ppermute | solution.py:74
  169.2 4.4 copy-start.1
  173.6 1.5 copy-start.2
  173.6 1.5 copy-start.3
  173.6 1.5 copy-start.4
  221.5 21.5 %collective-permute-start = (f32[1,2,110,256]{3,2,1,0:T(8,128)}, f32[1,2,110,256]{3,2,1,0:T(8,128)}, u32[]{:S(2)}, u32[]{:S(2)}) collective-permute-start(f32[1,2,110,256]{3,2,1,0:T(8,128)} %get-tuple-element.367), channel_id=1, source_target_pairs={{1,0},{2,1},{3,2},{4,3},{5,4},{6,5},{7,6},{8,7},{9,8},{10,9},{11,1... | collective-permute-start | bytes 675848 | tf_op jit(solution)/shard_map/while/body/eval_jaxpr/ppermute | solution.py:75
  227.2 15.8 %collective-permute-start.1 = (f32[1,2,110,256]{3,2,1,0:T(8,128)}, f32[1,2,110,256]{3,2,1,0:T(8,128)}, u32[]{:S(2)}, u32[]{:S(2)}) collective-permute-start(f32[1,2,110,256]{3,2,1,0:T(8,128)} %get-tuple-element.367), channel_id=1, source_target_pairs={{0,1},{1,2},{2,3},{3,4},{4,5},{5,6},{6,7},{7,8},{8,9},{9,10},{10,1... | collective-permute-start | bytes 675848 | tf_op jit(solution)/shard_map/while/body/eval_jaxpr/ppermute | solution.py:74
  236.8 4.4 copy-start.1
  241.1 1.5 copy-start.2
  241.1 1.5 copy-start.3
  241.2 1.5 copy-start.4
  289.0 21.5 %collective-permute-start = (f32[1,2,110,256]{3,2,1,0:T(8,128)}, f32[1,2,110,256]{3,2,1,0:T(8,128)}, u32[]{:S(2)}, u32[]{:S(2)}) collective-permute-start(f32[1,2,110,256]{3,2,1,0:T(8,128)} %get-tuple-element.367), channel_id=1, source_target_pairs={{1,0},{2,1},{3,2},{4,3},{5,4},{6,5},{7,6},{8,7},{9,8},{10,9},{11,1... | collective-permute-start | bytes 675848 | tf_op jit(solution)/shard_map/while/body/eval_jaxpr/ppermute | solution.py:75
  294.8 15.8 %collective-permute-start.1 = (f32[1,2,110,256]{3,2,1,0:T(8,128)}, f32[1,2,110,256]{3,2,1,0:T(8,128)}, u32[]{:S(2)}, u32[]{:S(2)}) collective-permute-start(f32[1,2,110,256]{3,2,1,0:T(8,128)} %get-tuple-element.367), channel_id=1, source_target_pairs={{0,1},{1,2},{2,3},{3,4},{4,5},{5,6},{6,7},{7,8},{8,9},{9,10},{10,1... | collective-permute-start | bytes 675848 | tf_op jit(solution)/shard_map/while/body/eval_jaxpr/ppermute | solution.py:74
  304.3 4.4 copy-start.1
  308.7 1.5 copy-start.2
  308.7 1.5 copy-start.3
  308.7 1.5 copy-start.4
  356.6 21.5 %collective-permute-start = (f32[1,2,110,256]{3,2,1,0:T(8,128)}, f32[1,2,110,256]{3,2,1,0:T(8,128)}, u32[]{:S(2)}, u32[]{:S(2)}) collective-permute-start(f32[1,2,110,256]{3,2,1,0:T(8,128)} %get-tuple-element.367), channel_id=1, source_target_pairs={{1,0},{2,1},{3,2},{4,3},{5,4},{6,5},{7,6},{8,7},{9,8},{10,9},{11,1... | collective-permute-start | bytes 675848 | tf_op jit(solution)/shard_map/while/body/eval_jaxpr/ppermute | solution.py:75
  362.3 15.8 %collective-permute-start.1 = (f32[1,2,110,256]{3,2,1,0:T(8,128)}, f32[1,2,110,256]{3,2,1,0:T(8,128)}, u32[]{:S(2)}, u32[]{:S(2)}) collective-permute-start(f32[1,2,110,256]{3,2,1,0:T(8,128)} %get-tuple-element.367), channel_id=1, source_target_pairs={{0,1},{1,2},{2,3},{3,4},{4,5},{5,6},{6,7},{7,8},{8,9},{9,10},{10,1... | collective-permute-start | bytes 675848 | tf_op jit(solution)/shard_map/while/body/eval_jaxpr/ppermute | solution.py:74
  371.9 4.4 copy-start.1
  376.2 1.5 copy-start.2
  376.2 1.5 copy-start.3
  376.2 1.5 copy-start.4
  424.1 21.5 %collective-permute-start = (f32[1,2,110,256]{3,2,1,0:T(8,128)}, f32[1,2,110,256]{3,2,1,0:T(8,128)}, u32[]{:S(2)}, u32[]{:S(2)}) collective-permute-start(f32[1,2,110,256]{3,2,1,0:T(8,128)} %get-tuple-element.367), channel_id=1, source_target_pairs={{1,0},{2,1},{3,2},{4,3},{5,4},{6,5},{7,6},{8,7},{9,8},{10,9},{11,1... | collective-permute-start | bytes 675848 | tf_op jit(solution)/shard_map/while/body/eval_jaxpr/ppermute | solution.py:75
  429.9 15.8 %collective-permute-start.1 = (f32[1,2,110,256]{3,2,1,0:T(8,128)}, f32[1,2,110,256]{3,2,1,0:T(8,128)}, u32[]{:S(2)}, u32[]{:S(2)}) collective-permute-start(f32[1,2,110,256]{3,2,1,0:T(8,128)} %get-tuple-element.367), channel_id=1, source_target_pairs={{0,1},{1,2},{2,3},{3,4},{4,5},{5,6},{6,7},{7,8},{8,9},{9,10},{10,1... | collective-permute-start | bytes 675848 | tf_op jit(solution)/shard_map/while/body/eval_jaxpr/ppermute | solution.py:74
  439.4 4.4 copy-start.1
  443.8 1.5 copy-start.2
  443.8 1.5 copy-start.3
  443.8 1.5 copy-start.4
  491.7 21.5 %collective-permute-start = (f32[1,2,110,256]{3,2,1,0:T(8,128)}, f32[1,2,110,256]{3,2,1,0:T(8,128)}, u32[]{:S(2)}, u32[]{:S(2)}) collective-permute-start(f32[1,2,110,256]{3,2,1,0:T(8,128)} %get-tuple-element.367), channel_id=1, source_target_pairs={{1,0},{2,1},{3,2},{4,3},{5,4},{6,5},{7,6},{8,7},{9,8},{10,9},{11,1... | collective-permute-start | bytes 675848 | tf_op jit(solution)/shard_map/while/body/eval_jaxpr/ppermute | solution.py:75
  497.4 15.8 %collective-permute-start.1 = (f32[1,2,110,256]{3,2,1,0:T(8,128)}, f32[1,2,110,256]{3,2,1,0:T(8,128)}, u32[]{:S(2)}, u32[]{:S(2)}) collective-permute-start(f32[1,2,110,256]{3,2,1,0:T(8,128)} %get-tuple-element.367), channel_id=1, source_target_pairs={{0,1},{1,2},{2,3},{3,4},{4,5},{5,6},{6,7},{7,8},{8,9},{9,10},{10,1... | collective-permute-start | bytes 675848 | tf_op jit(solution)/shard_map/while/body/eval_jaxpr/ppermute | solution.py:74
  506.9 4.4 copy-start.1
  511.3 1.5 copy-start.2
  511.3 1.5 copy-start.3
  511.3 1.5 copy-start.4
  559.2 21.5 %collective-permute-start = (f32[1,2,110,256]{3,2,1,0:T(8,128)}, f32[1,2,110,256]{3,2,1,0:T(8,128)}, u32[]{:S(2)}, u32[]{:S(2)}) collective-permute-start(f32[1,2,110,256]{3,2,1,0:T(8,128)} %get-tuple-element.367), channel_id=1, source_target_pairs={{1,0},{2,1},{3,2},{4,3},{5,4},{6,5},{7,6},{8,7},{9,8},{10,9},{11,1... | collective-permute-start | bytes 675848 | tf_op jit(solution)/shard_map/while/body/eval_jaxpr/ppermute | solution.py:75
  565.0 15.8 %collective-permute-start.1 = (f32[1,2,110,256]{3,2,1,0:T(8,128)}, f32[1,2,110,256]{3,2,1,0:T(8,128)}, u32[]{:S(2)}, u32[]{:S(2)}) collective-permute-start(f32[1,2,110,256]{3,2,1,0:T(8,128)} %get-tuple-element.367), channel_id=1, source_target_pairs={{0,1},{1,2},{2,3},{3,4},{4,5},{5,6},{6,7},{7,8},{8,9},{9,10},{10,1... | collective-permute-start | bytes 675848 | tf_op jit(solution)/shard_map/while/body/eval_jaxpr/ppermute | solution.py:74
  574.5 4.4 copy-start.1
  578.9 1.5 copy-start.2
  578.9 1.5 copy-start.3
  578.9 1.5 copy-start.4
  626.7 4.0 copy-start.5
Sparse Core Ops, SparseCore 0:
  9.9 74.1 all-gather.1
